TPU v7x, 256 devices: a whole 4x4x8 slice. The times are simulated.
256 devices in a mesh: tm: 4 (over y), row: 4 (over x), col: 16 (over z, core).
Axes of the slice: x: 4, y: 4, z: 8, core: 2. Of those that a mesh axis runs over, the one named last changes fastest.
Arguments:
- day_block: float32 [4, 4, 16, 32, 4, 4, 128], P('tm', None, 'col', None, None, 'row'), as said below
- left_coupling: float32 [4, 4, 16, 32, 4, 4, 128], P('tm', None, 'col', None, None, 'row'), may hold values from -0.125 to 0.125
- right_coupling: float32 [4, 4, 16, 32, 4, 4, 128], P('tm', None, 'col', None, None, 'row'), may hold values from -0.125 to 0.125
- separator_block: float32 [4, 4, 16, 32, 4, 4, 128], P('tm', None, 'col', None, None, 'row')
- arrow_coupling: float32 [4, 4, 16, 32, 64], P('tm', None, 'col'), may hold values from -0.125 to 0.125
- arrow_block: float32 [64, 64], replicated
Outputs:
- day_factor: float32 [4, 4, 16, 32, 4, 4, 128], P('tm', None, 'col', None, None, 'row')
- left_factor: float32 [4, 4, 16, 32, 4, 4, 128], P('tm', None, 'col', None, None, 'row')
- right_factor: float32 [4, 4, 16, 32, 4, 4, 128], P('tm', None, 'col', None, None, 'row')
- arrow_factor: float32 [4, 4, 16, 32, 64], P('tm', None, 'col')
- separator: float32 [4, 4, 16, 32, 4, 4, 128], P('tm', None, 'col', None, None, 'row')
- arrowhead: float32 [64, 64], replicated
Inputs may be any that keep to these rules, and one draw needn't show every extreme that they name: Each group's day_block and separator_block, and arrow_block, is an exactly symmetric matrix with all eigenvalues at least 1.
All inputs are finite; a program needn't handle non-finite values.
Results may differ from a plain program's by a relative error of at most 0.0001.
Values sent between devices are 32-bit elements; how exact they have to be, the bound alone decides.
No kernel may reach another device: no remote copies, remote signals or barrier semaphores. Data moves between devices by JAX's collectives and lax.ppermute only.
A program may use at most 128 MiB of HBM per device.

v0:
```python
import jax
import jax.numpy as jnp
from jax import lax
from jax.sharding import PartitionSpec as P


def passed_along(value, axis, steps):
    count = lax.axis_size(axis)
    initial, last = (max(0, -steps), min(count, count - steps))
    return lax.ppermute(value, axis, [(source, source + steps) for source in range(initial, last)])


def product(left, right):
    return jnp.dot(left, right, precision=lax.Precision.HIGHEST, preferred_element_type=jnp.float32)


def lower_inverse(factor):
    identity = jnp.eye(factor.shape[0], dtype=jnp.float32)
    return lax.linalg.triangular_solve(factor, identity, left_side=True, lower=True)


def reorder_nodes(whole, panels, col_width):
    count = whole.shape[0]
    col_count = lax.axis_size("col")
    spread = whole.reshape(count, panels, col_count, col_width)
    return jnp.transpose(spread, (2, 1, 3, 0)).reshape(col_count * panels * col_width, count)


def separator_term(solved, panels, col_width, row_width):
    whole = lax.all_gather(
        solved.reshape(solved.shape[0], panels, 1, row_width), "row", axis=2, tiled=True
    )
    ordered = reorder_nodes(whole, panels, col_width)
    return lax.psum_scatter(product(ordered, solved), "col", scatter_dimension=0, tiled=True)


def per_device(
    day_block, left_coupling, right_coupling, separator_block, arrow_coupling, arrow_block
):
    panels = day_block.shape[1]
    col_width = day_block.shape[3]
    row_width = day_block.shape[6]
    panel_size = col_width * lax.axis_size("col")
    arrow_rows = arrow_block.shape[0]
    col_index = lax.axis_index("col")
    row_index = lax.axis_index("row")
    matrix = day_block.reshape(panels, col_width, panels, row_width)
    left_part = left_coupling.reshape(panels, col_width, panels, row_width)
    right_part = right_coupling.reshape(panels, col_width, panels, row_width)
    arrow_part = arrow_coupling.reshape(panels, col_width, arrow_rows)
    rows_at = col_index * col_width + lax.broadcasted_iota(jnp.int32, (col_width, row_width), 0)
    cols_at = row_index * row_width + lax.broadcasted_iota(jnp.int32, (col_width, row_width), 1)
    factor_blocks = []
    left_blocks = []
    right_blocks = []
    arrow_blocks = []
    for current in range(panels):
        remain = panels - current
        gathered_day, gathered_left, gathered_right, gathered_arrow = (
            lax.all_gather(matrix[current, :, current:, :], "col", axis=0, tiled=True),
            lax.all_gather(left_part[current], "col", axis=0, tiled=True),
            lax.all_gather(right_part[current], "col", axis=0, tiled=True),
            lax.all_gather(arrow_part[current], "col", axis=0, tiled=True),
        )
        diagonal_full = lax.all_gather(gathered_day[:, 0:1, :], "row", axis=1, tiled=True).reshape(
            panel_size, panel_size
        )
        factor = jnp.linalg.cholesky(diagonal_full)
        inverse = lower_inverse(factor)
        owned = product(inverse, gathered_day.reshape(panel_size, remain * row_width)).reshape(
            panel_size, remain, row_width
        )
        if remain > 1:
            later = lax.all_gather(owned[:, 1:, None, :], "row", axis=2, tiled=True).reshape(
                panel_size, remain - 1, panel_size
            )
        solved_left = product(inverse, gathered_left.reshape(panel_size, panels * row_width))
        solved_right = product(inverse, gathered_right.reshape(panel_size, panels * row_width))
        solved_arrow = product(inverse, gathered_arrow)
        mine_rows = lax.dynamic_slice_in_dim(owned, col_index * col_width, col_width, 0)
        diagonal_part = jnp.where(cols_at >= rows_at, mine_rows[:, 0, :], 0.0)
        factor_blocks.append(
            jnp.concatenate(
                [
                    jnp.zeros((col_width, current, row_width), jnp.float32),
                    diagonal_part[:, None, :],
                    mine_rows[:, 1:, :],
                ],
                axis=1,
            )
        )
        left_blocks.append(
            lax.dynamic_slice_in_dim(solved_left, col_index * col_width, col_width, 0)
        )
        right_blocks.append(
            lax.dynamic_slice_in_dim(solved_right, col_index * col_width, col_width, 0)
        )
        arrow_blocks.append(
            lax.dynamic_slice_in_dim(solved_arrow, col_index * col_width, col_width, 0)
        )
        if remain > 1:
            mine_later = lax.dynamic_slice_in_dim(later, col_index * col_width, col_width, 2)
            mine_later = mine_later.reshape(panel_size, (remain - 1) * col_width).T
            owned_later = owned[:, 1:, :].reshape(panel_size, (remain - 1) * row_width)
            matrix = matrix.at[current + 1 :, :, current + 1 :, :].add(
                -product(mine_later, owned_later).reshape(
                    remain - 1, col_width, remain - 1, row_width
                )
            )
            left_part = left_part.at[current + 1 :].add(
                -product(mine_later, solved_left).reshape(remain - 1, col_width, panels, row_width)
            )
            right_part = right_part.at[current + 1 :].add(
                -product(mine_later, solved_right).reshape(remain - 1, col_width, panels, row_width)
            )
            arrow_part = arrow_part.at[current + 1 :].add(
                -product(mine_later, solved_arrow).reshape(remain - 1, col_width, arrow_rows)
            )
    day_factor = jnp.stack(factor_blocks).reshape(day_block.shape)
    left_solved = jnp.stack(left_blocks).reshape(panels * col_width, panels * row_width)
    right_solved = jnp.stack(right_blocks).reshape(panels * col_width, panels * row_width)
    arrow_solved = jnp.stack(arrow_blocks).reshape(panels * col_width, arrow_rows)
    separator_local = separator_block.reshape(panels * col_width, panels * row_width)
    right_term = separator_term(right_solved, panels, col_width, row_width)
    left_term = separator_term(left_solved, panels, col_width, row_width)
    from_next = passed_along(left_term, "tm", -1)
    separator = separator_local - right_term - from_next
    arrow_local = product(arrow_solved.T, arrow_solved)
    arrow_local = jnp.where(row_index == 0, arrow_local, 0.0)
    arrow_total = lax.psum(arrow_local, ("tm", "row", "col"))
    arrowhead = arrow_block - arrow_total
    return (
        day_factor,
        left_solved.reshape(left_coupling.shape),
        right_solved.reshape(right_coupling.shape),
        arrow_solved.reshape(arrow_coupling.shape),
        separator.reshape(separator_block.shape),
        arrowhead,
    )


def solution(mesh):
    return jax.shard_map(
        per_device,
        mesh=mesh,
        in_specs=(
            P("tm", None, "col", None, None, "row", None),
            P("tm", None, "col", None, None, "row", None),
            P("tm", None, "col", None, None, "row", None),
            P("tm", None, "col", None, None, "row", None),
            P("tm", None, "col", None, None),
            P(),
        ),
        out_specs=(
            P("tm", None, "col", None, None, "row", None),
            P("tm", None, "col", None, None, "row", None),
            P("tm", None, "col", None, None, "row", None),
            P("tm", None, "col", None, None),
            P("tm", None, "col", None, None, "row", None),
            P(),
        ),
        check_vma=False,
    )
```

profile of v0, /device:TPU:1, one launch (start us, length us, event | category | flops | bytes accessed | tf_op | source)
XLA Modules:
  0.0 1345.4 jit_solution(15966232665213219999)
XLA Ops:
  8.8 44.4 %all-gather.49.cloned.1.call-done = f32[1,1,1,512,4,1,128]{6,4,5,2,1,0,3:T(4,128)} async-done(((f32[1,1,1,32,4,1,128]{6,4,5,2,1,0,3:T(4,128)}), f32[1,1,1,512,4,1,128]{6,4,5,2,1,0,3:T(4,128)}) %all-gather.49.cloned.1.call-update) | async-done | bytes 1048592 | tf_op jit(solution)/shard_map/all_gather | solution.py:60
  58.0 20.3 %all-gather.39.cloned.1.call-done = f32[512,4,128]{2,0,1:T(8,128)} async-done(((f32[512,1,128]{2,0,1:T(8,128)}), f32[512,4,128]{2,0,1:T(8,128)}) %all-gather.39.cloned.1.call-update) | async-done | bytes 1048592 | tf_op jit(solution)/shard_map/all_gather | solution.py:65
  176.8 39.3 %custom-call.38 = f32[4,128,128]{1,2,0:T(8,128)S(1)} custom-call(f32[4,128,128]{2,1,0:T(8,128)S(1)} %get-tuple-element.178), custom_call_target="InvertDiagBlocksLowerTriangular" | custom-call | tf_op jit(solution)/shard_map/triangular_solve/custom-call.3 | solution.py:19
  227.9 44.9 %all-gather.51.cloned.1.call-done = f32[512,3,512]{2,0,1:T(8,128)} async-done(((f32[512,3,128]{2,0,1:T(8,128)}), f32[512,3,512]{2,0,1:T(8,128)}) %all-gather.51.cloned.1.call-update) | async-done | bytes 3145744 | tf_op jit(solution)/shard_map/all_gather | solution.py:74
  278.0 21.4 %all-gather.2 = f32[1,512,3,128]{3,1,2,0:T(8,128)S(1)} all-gather(f32[1,32,3,128]{3,1,2,0:T(8,128)S(1)} %slice.678), channel_id=4, replica_groups=mesh['tm'=4,'row'=4,'col'=16] {'col'}, dimensions={1}, use_global_device_ids=true | all-gather | bytes 835584 | tf_op jit(solution)/shard_map/all_gather | solution.py:60
  301.6 21.1 %all-gather.41.cloned.1.call-done = f32[512,4,128]{2,0,1:T(8,128)} async-done(((f32[512,1,128]{2,0,1:T(8,128)}), f32[512,4,128]{2,0,1:T(8,128)}) %all-gather.41.cloned.1.call-update) | async-done | bytes 1048592 | tf_op jit(solution)/shard_map/all_gather | solution.py:65
  428.6 39.3 %custom-call.42 = f32[4,128,128]{1,2,0:T(8,128)S(1)} custom-call(f32[4,128,128]{2,1,0:T(8,128)S(1)} %get-tuple-element.179), custom_call_target="InvertDiagBlocksLowerTriangular" | custom-call | tf_op jit(solution)/shard_map/triangular_solve/custom-call.3 | solution.py:19
  485.3 32.5 %all-gather.53.cloned.1.call-done = f32[512,2,512]{2,0,1:T(8,128)} async-done(((f32[512,2,128]{2,0,1:T(8,128)}), f32[512,2,512]{2,0,1:T(8,128)}) %all-gather.53.cloned.1.call-update) | async-done | bytes 2097168 | tf_op jit(solution)/shard_map/all_gather | solution.py:74
  522.9 20.8 %all-gather.4 = f32[1,512,2,128]{3,1,2,0:T(8,128)S(1)} all-gather(f32[1,32,2,128]{3,1,2,0:T(8,128)S(1)} %slice.689), channel_id=6, replica_groups=mesh['tm'=4,'row'=4,'col'=16] {'col'}, dimensions={1}, use_global_device_ids=true | all-gather | bytes 557056 | tf_op jit(solution)/shard_map/all_gather | solution.py:60
  545.3 16.1 %all-gather.59.cloned.1.call-done = f32[1,1,1,512,4,1,128]{6,4,5,2,1,0,3:T(4,128)} async-done(((f32[1,1,1,32,4,1,128]{6,4,5,2,1,0,3:T(4,128)}), f32[1,1,1,512,4,1,128]{6,4,5,2,1,0,3:T(4,128)}) %all-gather.59.cloned.1.call-update) | async-done | bytes 1048592 | tf_op jit(solution)/shard_map/all_gather | solution.py:61
  572.7 27.8 %all-gather.67.cloned.1.call-done = f32[1,1,1,512,4,1,128]{6,4,5,2,1,0,3:T(4,128)} async-done(((f32[1,1,1,32,4,1,128]{6,4,5,2,1,0,3:T(4,128)}), f32[1,1,1,512,4,1,128]{6,4,5,2,1,0,3:T(4,128)}) %all-gather.67.cloned.1.call-update) | async-done | bytes 1048592 | tf_op jit(solution)/shard_map/all_gather | solution.py:62
  612.0 13.6 %all-gather.43.cloned.1.call-done = f32[512,4,128]{2,0,1:T(8,128)} async-done(((f32[512,1,128]{2,0,1:T(8,128)}), f32[512,4,128]{2,0,1:T(8,128)}) %all-gather.43.cloned.1.call-update) | async-done | bytes 1048592 | tf_op jit(solution)/shard_map/all_gather | solution.py:65
  732.6 39.3 %custom-call.46 = f32[4,128,128]{1,2,0:T(8,128)S(1)} custom-call(f32[4,128,128]{2,1,0:T(8,128)S(1)} %get-tuple-element.180), custom_call_target="InvertDiagBlocksLowerTriangular" | custom-call | tf_op jit(solution)/shard_map/triangular_solve/custom-call.3 | solution.py:19
  815.0 22.1 %all-gather.6 = f32[1,512,1,128]{3,1,2,0:T(8,128)} all-gather(f32[1,32,1,128]{3,1,2,0:T(8,128)S(1)} %fusion.16), channel_id=8, replica_groups=mesh['tm'=4,'row'=4,'col'=16] {'col'}, dimensions={1}, use_global_device_ids=true | all-gather | bytes 278528 | tf_op jit(solution)/shard_map/all_gather | solution.py:60
  837.2 17.1 %all-gather.63.cloned.1.call-done = f32[1,512,4,128]{3,1,2,0:T(8,128)} async-done(((f32[1,32,4,128]{3,1,2,0:T(8,128)}), f32[1,512,4,128]{3,1,2,0:T(8,128)}) %all-gather.63.cloned.1.call-update) | async-done | bytes 1048592 | tf_op jit(solution)/shard_map/all_gather | solution.py:61
  869.4 24.0 %all-gather.71.cloned.1.call-done = f32[1,512,4,128]{3,1,2,0:T(8,128)} async-done(((f32[1,32,4,128]{3,1,2,0:T(8,128)}), f32[1,512,4,128]{3,1,2,0:T(8,128)}) %all-gather.71.cloned.1.call-update) | async-done | bytes 1048592 | tf_op jit(solution)/shard_map/all_gather | solution.py:62
  1041.1 39.3 %custom-call.50 = f32[4,128,128]{1,2,0:T(8,128)S(1)} custom-call(f32[4,128,128]{2,1,0:T(8,128)S(1)} %get-tuple-element.181), custom_call_target="InvertDiagBlocksLowerTriangular" | custom-call | tf_op jit(solution)/shard_map/triangular_solve/custom-call.3 | solution.py:19
  1105.2 16.4 %all-gather.47.cloned.1.call-done = f32[128,4,4,128]{3,0,1,2:T(8,128)} async-done(((f32[128,4,1,128]{3,0,1,2:T(8,128)}), f32[128,4,4,128]{3,0,1,2:T(8,128)}) %all-gather.47.cloned.1.call-update) | async-done | bytes 1048592 | tf_op jit(solution)/shard_map/all_gather | solution.py:30
  1128.5 21.8 %all-gather.45.cloned.1.call-done = f32[128,4,4,128]{3,0,1,2:T(8,128)} async-done(((f32[128,4,1,128]{3,0,1,2:T(8,128)}), f32[128,4,4,128]{3,0,1,2:T(8,128)}) %all-gather.45.cloned.1.call-update) | async-done | bytes 1048592 | tf_op jit(solution)/shard_map/all_gather | solution.py:30
  1157.6 20.8 %all-gather.16 = f32[1,1,1,512,64]{4,3,2,1,0:T(8,128)S(1)} all-gather(f32[1,1,1,32,64]{4,3,2,1,0:T(8,128)S(1)} %slice-done.1), channel_id=18, replica_groups=mesh['tm'=4,'row'=4,'col'=16] {'col'}, dimensions={3}, use_global_device_ids=true | all-gather | bytes 139264 | tf_op jit(solution)/shard_map/all_gather | solution.py:63
  1187.4 15.8 %all-gather.17 = f32[1,512,64]{2,1,0:T(8,128)S(1)} all-gather(f32[1,32,64]{2,1,0:T(8,128)S(1)} %slice.716), channel_id=19, replica_groups=mesh['tm'=4,'row'=4,'col'=16] {'col'}, dimensions={1}, use_global_device_ids=true | all-gather | bytes 139264 | tf_op jit(solution)/shard_map/all_gather | solution.py:63
  1208.7 16.2 %all-gather.18 = f32[1,512,64]{2,1,0:T(8,128)S(1)} all-gather(f32[1,32,64]{2,1,0:T(8,128)S(1)} %slice.718), channel_id=20, replica_groups=mesh['tm'=4,'row'=4,'col'=16] {'col'}, dimensions={1}, use_global_device_ids=true | all-gather | bytes 139264 | tf_op jit(solution)/shard_map/all_gather | solution.py:63
  1230.8 16.0 %all-gather.19 = f32[1,512,64]{2,1,0:T(8,128)S(1)} all-gather(f32[1,32,64]{2,1,0:T(8,128)S(1)} %fusion.14), channel_id=21, replica_groups=mesh['tm'=4,'row'=4,'col'=16] {'col'}, dimensions={1}, use_global_device_ids=true | all-gather | bytes 139264 | tf_op jit(solution)/shard_map/all_gather | solution.py:63
  1250.3 74.9 %psum.7 = f32[64,64]{1,0:T(8,128)S(1)} all-reduce(f32[64,64]{1,0:T(8,128)S(1)} %fusion.12), channel_id=1, replica_groups=mesh['tm'=4,'row'=4,'col'=16] {'tm','row','col'}, use_global_device_ids=true, to_apply=%region_10.0 | all-reduce | flops 4096 | bytes 32768 | tf_op jit(solution)/shard_map/psum | solution.py:130
  (518 shorter events, 695.8 us)
Async XLA Ops:
  7.2 46.0 %all-gather.49.cloned.1.call-start = ((), (), s32[]{:S(2)}) async-start(), calls=%async_computation.9 | async-start | bytes 1114112 | tf_op jit(solution)/shard_map/all_gather | solution.py:60
  8.7 69.5 %all-gather.39.cloned.1.call-start = ((), (), s32[]{:S(2)}) async-start(), calls=%async_computation.2 | async-start | bytes 1310720 | tf_op jit(solution)/shard_map/all_gather | solution.py:65
  55.3 217.5 %all-gather.51.cloned.1.call-start = ((), (), s32[]{:S(2)}) async-start(), calls=%async_computation.10 | async-start | bytes 3932160 | tf_op jit(solution)/shard_map/all_gather | solution.py:74
  219.1 381.4 %copy-start = (f32[128,512]{1,0:T(8,128)}, f32[128,512]{1,0:T(8,128)S(1)}, u32[]{:S(2)}) copy-start(f32[128,512]{1,0:T(8,128)S(1)} %fusion.152) | copy-start | bytes 786436
  226.3 96.4 %all-gather.41.cloned.1.call-start = ((), (), s32[]{:S(2)}) async-start(), calls=%async_computation.3 | async-start | bytes 1310720 | tf_op jit(solution)/shard_map/all_gather | solution.py:65
  276.4 329.7 %copy-start.9 = (f32[512,3,32]{0,2,1:T(8,128)}, f32[512,3,32]{0,2,1:T(8,128)S(1)}, u32[]{:S(2)}) copy-start(f32[512,3,32]{0,2,1:T(8,128)S(1)} %copy.124) | copy-start | bytes 589828
  300.2 217.7 %all-gather.53.cloned.1.call-start = ((), (), s32[]{:S(2)}) async-start(), calls=%async_computation.11 | async-start | bytes 2621440 | tf_op jit(solution)/shard_map/all_gather | solution.py:74
  480.1 81.3 %all-gather.59.cloned.1.call-start = ((), (), s32[]{:S(2)}) async-start(), calls=%async_computation.14 | async-start | bytes 1114112 | tf_op jit(solution)/shard_map/all_gather | solution.py:61
  481.7 118.8 %all-gather.67.cloned.1.call-start = ((), (), s32[]{:S(2)}) async-start(), calls=%async_computation.18 | async-start | bytes 1114112 | tf_op jit(solution)/shard_map/all_gather | solution.py:62
  483.2 142.4 %all-gather.43.cloned.1.call-start = ((), (), s32[]{:S(2)}) async-start(), calls=%async_computation.4 | async-start | bytes 1310720 | tf_op jit(solution)/shard_map/all_gather | solution.py:65
  545.2 238.8 %all-gather.61.cloned.1.call-start = ((), (), s32[]{:S(2)}) async-start(), calls=%async_computation.15 | async-start | bytes 1114112 | tf_op jit(solution)/shard_map/all_gather | solution.py:61
  571.1 226.4 %all-gather.69.cloned.1.call-start = ((), (), s32[]{:S(2)}) async-start(), calls=%async_computation.19 | async-start | bytes 1114112 | tf_op jit(solution)/shard_map/all_gather | solution.py:62
  609.5 201.7 %all-gather.55.cloned.1.call-start = ((), (), s32[]{:S(2)}) async-start(), calls=%async_computation.12 | async-start | bytes 1310720 | tf_op jit(solution)/shard_map/all_gather | solution.py:74
  774.0 121.9 %copy-start.5 = (f32[128,512]{1,0:T(8,128)}, f32[128,512]{1,0:T(8,128)S(1)}, u32[]{:S(2)}) copy-start(f32[128,512]{1,0:T(8,128)S(1)} %fusion.142) | copy-start | bytes 786436
  784.0 70.3 %all-gather.63.cloned.1.call-start = ((), (), s32[]{:S(2)}) async-start(), calls=%async_computation.16 | async-start | bytes 1114112 | tf_op jit(solution)/shard_map/all_gather | solution.py:61
  796.9 96.4 %all-gather.71.cloned.1.call-start = ((), (), s32[]{:S(2)}) async-start(), calls=%async_computation.20 | async-start | bytes 1114112 | tf_op jit(solution)/shard_map/all_gather | solution.py:62
  809.7 108.1 %all-gather.57.cloned.1.call-start = ((), (), s32[]{:S(2)}) async-start(), calls=%async_computation.13 | async-start | bytes 1310720 | tf_op jit(solution)/shard_map/all_gather | solution.py:65
  837.1 251.1 %all-gather.65.cloned.1.call-start = ((), (), s32[]{:S(2)}) async-start(), calls=%async_computation.17 | async-start | bytes 1114112 | tf_op jit(solution)/shard_map/all_gather | solution.py:61
  866.4 232.6 %all-gather.73.cloned.1.call-start = ((), (), s32[]{:S(2)}) async-start(), calls=%async_computation.21 | async-start | bytes 1114112 | tf_op jit(solution)/shard_map/all_gather | solution.py:62
  905.6 216.0 %all-gather.47.cloned.1.call-start = ((), (), s32[]{:S(2)}) async-start(), calls=%async_computation.7 | async-start | bytes 1310720 | tf_op jit(solution)/shard_map/all_gather | solution.py:30
  1094.5 55.9 %all-gather.45.cloned.1.call-start = ((), (), s32[]{:S(2)}) async-start(), calls=%async_computation.5 | async-start | bytes 1310720 | tf_op jit(solution)/shard_map/all_gather | solution.py:30
  1105.2 222.1 %reduce-scatter.5.cloned.1.call-start = ((), (), s32[]{:S(2)}) async-start(), calls=%async_computation.8 | async-start | bytes 4456448 | tf_op jit(solution)/shard_map/reduce_scatter | solution.py:34
  1128.3 203.2 %reduce-scatter.3.cloned.1.call-start = ((), (), s32[]{:S(2)}) async-start(), calls=%async_computation.6 | async-start | bytes 4456448 | tf_op jit(solution)/shard_map/reduce_scatter | solution.py:34
  1327.3 9.3 collective-permute-start
  (63 other events, 1884.1 us)
Sparse Core Ops, SparseCore 0:
  10.4 42.7 all-gather.48
  55.5 22.6 all-gather.38
  226.5 46.2 all-gather.50
  300.3 22.3 all-gather.40
  480.3 37.5 all-gather.52
  520.1 41.2 all-gather.58
  563.2 37.2 all-gather.66
  602.9 22.6 all-gather.42
  627.5 41.9 all-gather.60
  671.1 37.1 all-gather.68
  784.1 26.9 all-gather.54
  812.9 41.3 all-gather.62
  856.1 37.2 all-gather.70
  895.0 22.7 all-gather.56
  919.5 41.7 all-gather.64
  963.0 37.2 all-gather.72
  1094.6 26.9 all-gather.46
  1123.3 27.0 all-gather.44
  1152.9 63.7 reduce-scatter.4
  1219.1 62.5 reduce-scatter.2
where the time goes:
time: 1360 us; the launch traced here: 1350 us
  other arithmetic  503 us (37%)
  waiting for transfers between devices  319 us (23%)
  blocking collectives  208 us (15%)
  local copies, waits for them, and re-layouts  159 us (12%)
  matrix products  126 us (9%)
  between operations  26.5 us (2%)
    another operation x59, other arithmetic, per_device(): factor = jnp.linalg.cholesky(diagonal_full)  329 us
    another operation x9, other arithmetic, lower_inverse(): lax.linalg.triangular_solve(factor, identity, left_side=True, lower=True)  161 us
    all_gather x3, waiting for transfers between devices, per_device(): lax.all_gather(owned[:, 1:, None, :], 'row', axis=2, tiled=True)  78.9 us
    psum x1, blocking collectives, per_device(): arrow_total = lax.psum(arrow_local, ('tm', 'row', 'col'))  74.9 us
    dot_general x31, matrix products, product(): jnp.dot(left, right, precision=lax.Precision.HIGHEST, preferred_element_t...  73.6 us
    all_gather x4, blocking collectives, per_device(): lax.all_gather(arrow_part[current], 'col', axis=0, tiled=True)  68.8 us
    all_gather x4, waiting for transfers between devices, per_device(): lax.all_gather(gathered_day[:, 0:1, :], 'row', axis=1, tiled=True)  66.9 us
    all_gather x3, blocking collectives, per_device(): lax.all_gather(matrix[current, :, current:, :], 'col', axis=0, tiled=True)  64.4 us
  transfers between devices with their start and end apart: 21, of which 15 were waited for; matrix products, arithmetic and copies ran while one was open for 35% of the time, Pallas kernels for 0%

commit v1 on v0

--- a/solution.py
+++ b/solution.py
@@ -58,7 +58,10 @@
         remain = panels - current
         gathered_day, gathered_left, gathered_right, gathered_arrow = (
             lax.all_gather(matrix[current, :, current:, :], "col", axis=0, tiled=True),
-            lax.all_gather(left_part[current], "col", axis=0, tiled=True),
+            jnp.concatenate(
+                lax.all_to_all(jnp.stack([left_part[current]] * lax.axis_size("col")), "col", 0, 0),
+                axis=0,
+            ),
             lax.all_gather(right_part[current], "col", axis=0, tiled=True),
             lax.all_gather(arrow_part[current], "col", axis=0, tiled=True),
         )

time: 1360 us -> 1290 us (0.949)
  waiting for transfers between devices: 319 us -> 208 us
  starting transfers between devices: 3.49 us -> 32.6 us
  blocking collectives: 208 us -> 225 us
    all_gather x4, waiting for transfers between devices: 51.8 us -> 8.54 us  [per_device(): lax.all_gather(right_part[current], 'col', axis=0, tiled=True)]
    all_gather x4 -> x0, waiting for transfers between devices: 33.3 us -> none  [per_device(): lax.all_gather(left_part[current], 'col', axis=0, tiled=True)]
    all_to_all x0 -> x4, starting transfers between devices: none -> 29.5 us  [per_device(): lax.all_to_all(jnp.stack([left_part[current]] * lax.axis_size('col')), 'c...]
    all_gather x4, waiting for transfers between devices: 66.9 us -> 44.7 us  [per_device(): lax.all_gather(gathered_day[:, 0:1, :], 'row', axis=1, tiled=True)]
    all_gather x3, blocking collectives: 64.4 us -> 80.8 us  [per_device(): lax.all_gather(matrix[current, :, current:, :], 'col', axis=0, tiled=True)]
  transfers between devices with their start and end apart: 21 -> 21, of which waited for: 15 -> 10; matrix products, arithmetic and copies ran while one was open for 35% -> 36% of each run, Pallas kernels for 0% -> 0%
where the time goes in v1:
time: 1290 us; the launch traced here: 1280 us
  other arithmetic  503 us (39%)
  blocking collectives  225 us (17%)
  waiting for transfers between devices  208 us (16%)
  local copies, waits for them, and re-layouts  154 us (12%)
  matrix products  127 us (10%)
  starting transfers between devices  32.6 us (3%)
  between operations  26.2 us (2%)
    another operation x59, other arithmetic, per_device(): factor = jnp.linalg.cholesky(diagonal_full)  329 us
    another operation x9, other arithmetic, lower_inverse(): lax.linalg.triangular_solve(factor, identity, left_side=True, lower=True)  161 us
    all_gather x3, blocking collectives, per_device(): lax.all_gather(matrix[current, :, current:, :], 'col', axis=0, tiled=True)  80.8 us
    psum x1, blocking collectives, per_device(): arrow_total = lax.psum(arrow_local, ('tm', 'row', 'col'))  75 us
    dot_general x31, matrix products, product(): jnp.dot(left, right, precision=lax.Precision.HIGHEST, preferred_element_t...  74.3 us
    all_gather x3, waiting for transfers between devices, per_device(): lax.all_gather(owned[:, 1:, None, :], 'row', axis=2, tiled=True)  69 us
    all_gather x4, blocking collectives, per_device(): lax.all_gather(arrow_part[current], 'col', axis=0, tiled=True)  68.8 us
    all_gather x4, waiting for transfers between devices, per_device(): lax.all_gather(gathered_day[:, 0:1, :], 'row', axis=1, tiled=True)  44.7 us
  transfers between devices with their start and end apart: 21, of which 10 were waited for; matrix products, arithmetic and copies ran while one was open for 36% of the time, Pallas kernels for 0%

profile of v1, /device:TPU:1, one launch (start us, length us, event | category | flops | bytes accessed | tf_op | source)
XLA Modules:
  0.0 1275.8 jit_solution(15707889670963329472)
XLA Ops:
  8.8 44.4 %all-gather.41.cloned.1.call-done = f32[1,1,1,512,4,1,128]{6,4,5,2,1,0,3:T(4,128)} async-done(((f32[1,1,1,32,4,1,128]{6,4,5,2,1,0,3:T(4,128)}), f32[1,1,1,512,4,1,128]{6,4,5,2,1,0,3:T(4,128)}) %all-gather.41.cloned.1.call-update) | async-done | bytes 1048592 | tf_op jit(solution)/shard_map/all_gather | solution.py:60
  58.0 20.3 %all-gather.31.cloned.1.call-done = f32[512,4,128]{2,0,1:T(8,128)} async-done(((f32[512,1,128]{2,0,1:T(8,128)}), f32[512,4,128]{2,0,1:T(8,128)}) %all-gather.31.cloned.1.call-update) | async-done | bytes 1048592 | tf_op jit(solution)/shard_map/all_gather | solution.py:68
  176.8 39.3 %custom-call.38 = f32[4,128,128]{1,2,0:T(8,128)S(1)} custom-call(f32[4,128,128]{2,1,0:T(8,128)S(1)} %get-tuple-element.178), custom_call_target="InvertDiagBlocksLowerTriangular" | custom-call | tf_op jit(solution)/shard_map/triangular_solve/custom-call.3 | solution.py:19
  227.9 44.9 %all-gather.43.cloned.1.call-done = f32[512,3,512]{2,0,1:T(8,128)} async-done(((f32[512,3,128]{2,0,1:T(8,128)}), f32[512,3,512]{2,0,1:T(8,128)}) %all-gather.43.cloned.1.call-update) | async-done | bytes 3145744 | tf_op jit(solution)/shard_map/all_gather | solution.py:77
  278.0 21.4 %all-gather.2 = f32[1,512,3,128]{3,1,2,0:T(8,128)S(1)} all-gather(f32[1,32,3,128]{3,1,2,0:T(8,128)S(1)} %slice.690), channel_id=4, replica_groups=mesh['tm'=4,'row'=4,'col'=16] {'col'}, dimensions={1}, use_global_device_ids=true | all-gather | bytes 835584 | tf_op jit(solution)/shard_map/all_gather | solution.py:60
  301.6 21.1 %all-gather.33.cloned.1.call-done = f32[512,4,128]{2,0,1:T(8,128)} async-done(((f32[512,1,128]{2,0,1:T(8,128)}), f32[512,4,128]{2,0,1:T(8,128)}) %all-gather.33.cloned.1.call-update) | async-done | bytes 1048592 | tf_op jit(solution)/shard_map/all_gather | solution.py:68
  428.5 39.3 %custom-call.42 = f32[4,128,128]{1,2,0:T(8,128)S(1)} custom-call(f32[4,128,128]{2,1,0:T(8,128)S(1)} %get-tuple-element.179), custom_call_target="InvertDiagBlocksLowerTriangular" | custom-call | tf_op jit(solution)/shard_map/triangular_solve/custom-call.3 | solution.py:19
  493.1 24.1 %all-gather.45.cloned.1.call-done = f32[512,2,512]{2,0,1:T(8,128)} async-done(((f32[512,2,128]{2,0,1:T(8,128)}), f32[512,2,512]{2,0,1:T(8,128)}) %all-gather.45.cloned.1.call-update) | async-done | bytes 2097168 | tf_op jit(solution)/shard_map/all_gather | solution.py:77
  520.3 20.7 %all-gather.4 = f32[1,512,2,128]{3,1,2,0:T(8,128)S(1)} all-gather(f32[1,32,2,128]{3,1,2,0:T(8,128)S(1)} %slice.701), channel_id=6, replica_groups=mesh['tm'=4,'row'=4,'col'=16] {'col'}, dimensions={1}, use_global_device_ids=true | all-gather | bytes 557056 | tf_op jit(solution)/shard_map/all_gather | solution.py:60
  665.0 11.9 cholesky.663
  681.3 12.0 while.22
  693.4 39.3 %custom-call.46 = f32[4,128,128]{1,2,0:T(8,128)S(1)} custom-call(f32[4,128,128]{2,1,0:T(8,128)S(1)} %get-tuple-element.180), custom_call_target="InvertDiagBlocksLowerTriangular" | custom-call | tf_op jit(solution)/shard_map/triangular_solve/custom-call.3 | solution.py:19
  781.5 38.6 %all-gather.6 = f32[1,512,1,128]{3,1,2,0:T(8,128)} all-gather(f32[1,32,1,128]{3,1,2,0:T(8,128)S(1)} %fusion.17), channel_id=8, replica_groups=mesh['tm'=4,'row'=4,'col'=16] {'col'}, dimensions={1}, use_global_device_ids=true | all-gather | bytes 278528 | tf_op jit(solution)/shard_map/all_gather | solution.py:60
  884.3 13.2 %cholesky.697 = f32[128,128]{1,0:T(8,128)} custom-call(f32[128,128]{1,0:T(8,128)} %cholesky.789), custom_call_target="Cholesky" | custom-call | tf_op jit(solution)/shard_map/jit(cholesky)/cholesky | solution.py:71
  914.9 13.2 %cholesky.718 = f32[128,128]{1,0:T(8,128)} custom-call(f32[128,128]{1,0:T(8,128)} %cholesky.794), custom_call_target="Cholesky" | custom-call | tf_op jit(solution)/shard_map/jit(cholesky)/cholesky | solution.py:71
  944.4 13.6 %cholesky.735 = f32[128,128]{1,0:T(8,128)} custom-call(f32[128,128]{1,0:T(8,128)} %convolution_subtract_fusion.20), custom_call_target="Cholesky" | custom-call | tf_op jit(solution)/shard_map/jit(cholesky)/cholesky | solution.py:71
  974.7 39.3 %custom-call.50 = f32[4,128,128]{1,2,0:T(8,128)S(1)} custom-call(f32[4,128,128]{2,1,0:T(8,128)S(1)} %get-tuple-element.181), custom_call_target="InvertDiagBlocksLowerTriangular" | custom-call | tf_op jit(solution)/shard_map/triangular_solve/custom-call.3 | solution.py:19
  1038.5 13.6 %all-gather.39.cloned.1.call-done = f32[128,4,4,128]{3,0,1,2:T(8,128)} async-done(((f32[128,4,1,128]{3,0,1,2:T(8,128)}), f32[128,4,4,128]{3,0,1,2:T(8,128)}) %all-gather.39.cloned.1.call-update) | async-done | bytes 1048592 | tf_op jit(solution)/shard_map/all_gather | solution.py:30
  1059.0 21.8 %all-gather.37.cloned.1.call-done = f32[128,4,4,128]{3,0,1,2:T(8,128)} async-done(((f32[128,4,1,128]{3,0,1,2:T(8,128)}), f32[128,4,4,128]{3,0,1,2:T(8,128)}) %all-gather.37.cloned.1.call-update) | async-done | bytes 1048592 | tf_op jit(solution)/shard_map/all_gather | solution.py:30
  1088.1 20.9 %all-gather.12 = f32[1,1,1,512,64]{4,3,2,1,0:T(8,128)S(1)} all-gather(f32[1,1,1,32,64]{4,3,2,1,0:T(8,128)S(1)} %slice-done.1), channel_id=14, replica_groups=mesh['tm'=4,'row'=4,'col'=16] {'col'}, dimensions={3}, use_global_device_ids=true | all-gather | bytes 139264 | tf_op jit(solution)/shard_map/all_gather | solution.py:66
  1118.0 15.7 %all-gather.13 = f32[1,512,64]{2,1,0:T(8,128)S(1)} all-gather(f32[1,32,64]{2,1,0:T(8,128)S(1)} %slice.728), channel_id=15, replica_groups=mesh['tm'=4,'row'=4,'col'=16] {'col'}, dimensions={1}, use_global_device_ids=true | all-gather | bytes 139264 | tf_op jit(solution)/shard_map/all_gather | solution.py:66
  1139.3 16.5 %all-gather.14 = f32[1,512,64]{2,1,0:T(8,128)S(1)} all-gather(f32[1,32,64]{2,1,0:T(8,128)S(1)} %slice.730), channel_id=16, replica_groups=mesh['tm'=4,'row'=4,'col'=16] {'col'}, dimensions={1}, use_global_device_ids=true | all-gather | bytes 139264 | tf_op jit(solution)/shard_map/all_gather | solution.py:66
  1161.7 15.8 %all-gather.15 = f32[1,512,64]{2,1,0:T(8,128)S(1)} all-gather(f32[1,32,64]{2,1,0:T(8,128)S(1)} %fusion.15), channel_id=17, replica_groups=mesh['tm'=4,'row'=4,'col'=16] {'col'}, dimensions={1}, use_global_device_ids=true | all-gather | bytes 139264 | tf_op jit(solution)/shard_map/all_gather | solution.py:66
  1180.9 75.0 %psum.7 = f32[64,64]{1,0:T(8,128)S(1)} all-reduce(f32[64,64]{1,0:T(8,128)S(1)} %fusion.13), channel_id=1, replica_groups=mesh['tm'=4,'row'=4,'col'=16] {'tm','row','col'}, use_global_device_ids=true, to_apply=%region_10.0 | all-reduce | flops 4096 | bytes 32768 | tf_op jit(solution)/shard_map/psum | solution.py:133
  (520 shorter events, 656.5 us)
Async XLA Ops:
  7.2 46.0 %all-gather.41.cloned.1.call-start = ((), (), s32[]{:S(2)}) async-start(), calls=%async_computation.13 | async-start | bytes 1114112 | tf_op jit(solution)/shard_map/all_gather | solution.py:60
  8.7 69.5 %all-gather.31.cloned.1.call-start = ((), (), s32[]{:S(2)}) async-start(), calls=%async_computation.6 | async-start | bytes 1310720 | tf_op jit(solution)/shard_map/all_gather | solution.py:68
  55.3 217.5 %all-gather.43.cloned.1.call-start = ((), (), s32[]{:S(2)}) async-start(), calls=%async_computation.14 | async-start | bytes 3932160 | tf_op jit(solution)/shard_map/all_gather | solution.py:77
  219.1 341.1 %copy-start = (f32[128,512]{1,0:T(8,128)}, f32[128,512]{1,0:T(8,128)S(1)}, u32[]{:S(2)}) copy-start(f32[128,512]{1,0:T(8,128)S(1)} %fusion.162) | copy-start | bytes 786436
  226.4 96.3 %all-gather.33.cloned.1.call-start = ((), (), s32[]{:S(2)}) async-start(), calls=%async_computation.7 | async-start | bytes 1310720 | tf_op jit(solution)/shard_map/all_gather | solution.py:68
  276.5 294.1 %copy-start.9 = (f32[512,3,32]{0,2,1:T(8,128)}, f32[512,3,32]{0,2,1:T(8,128)S(1)}, u32[]{:S(2)}) copy-start(f32[512,3,32]{0,2,1:T(8,128)S(1)} %copy.127) | copy-start | bytes 589828
  300.2 217.1 %all-gather.45.cloned.1.call-start = ((), (), s32[]{:S(2)}) async-start(), calls=%async_computation.15 | async-start | bytes 2621440 | tf_op jit(solution)/shard_map/all_gather | solution.py:77
  479.5 80.7 %all-gather.51.cloned.1.call-start = ((), (), s32[]{:S(2)}) async-start(), calls=%async_computation.18 | async-start | bytes 1114112 | tf_op jit(solution)/shard_map/all_gather | solution.py:65
  482.3 62.8 %all-to-all-start = ((f32[16,32,4,128]{3,2,1,0:T(4,128)}), f32[16,32,4,128]{3,2,1,0:T(4,128)}, u32[]{:S(2)}, u32[]{:S(2)}) async-start(f32[16,32,4,128]{3,2,1,0:T(4,128)} %stack.97), calls=%async_computation | async-start | bytes 2097152 | tf_op jit(solution)/shard_map/all_to_all | solution.py:62
  492.1 93.6 %all-gather.35.cloned.1.call-start = ((), (), s32[]{:S(2)}) async-start(), calls=%async_computation.8 | async-start | bytes 1310720 | tf_op jit(solution)/shard_map/all_gather | solution.py:68
  574.6 183.4 %all-to-all-start.1 = ((f32[16,32,4,128]{3,2,1,0:T(4,128)}), f32[16,32,4,128]{3,2,1,0:T(4,128)}, u32[]{:S(2)}, u32[]{:S(2)}) async-start(f32[16,32,4,128]{3,2,1,0:T(4,128)} %stack.99), calls=%async_computation.1 | async-start | bytes 2097152 | tf_op jit(solution)/shard_map/all_to_all | solution.py:62
  579.1 166.0 %all-gather.53.cloned.1.call-start = ((), (), s32[]{:S(2)}) async-start(), calls=%async_computation.19 | async-start | bytes 1114112 | tf_op jit(solution)/shard_map/all_gather | solution.py:65
  579.9 197.9 %all-gather.47.cloned.1.call-start = ((), (), s32[]{:S(2)}) async-start(), calls=%async_computation.16 | async-start | bytes 1310720 | tf_op jit(solution)/shard_map/all_gather | solution.py:77
  744.8 85.0 %all-gather.55.cloned.1.call-start = ((), (), s32[]{:S(2)}) async-start(), calls=%async_computation.20 | async-start | bytes 1114112 | tf_op jit(solution)/shard_map/all_gather | solution.py:65
  768.3 54.9 %all-to-all-start.2 = ((f32[16,32,4,128]{3,2,1,0:T(4,128)}), f32[16,32,4,128]{3,2,1,0:T(4,128)}, u32[]{:S(2)}, u32[]{:S(2)}) async-start(f32[16,32,4,128]{3,2,1,0:T(4,128)} %stack.101), calls=%async_computation.2 | async-start | bytes 2097152 | tf_op jit(solution)/shard_map/all_to_all | solution.py:62
  777.7 73.8 %all-gather.49.cloned.1.call-start = ((), (), s32[]{:S(2)}) async-start(), calls=%async_computation.17 | async-start | bytes 1310720 | tf_op jit(solution)/shard_map/all_gather | solution.py:68
  842.9 178.9 %all-to-all-start.3 = ((f32[16,32,4,128]{3,2,1,0:T(4,128)}), f32[16,32,4,128]{3,2,1,0:T(4,128)}, u32[]{:S(2)}, u32[]{:S(2)}) async-start(f32[16,32,4,128]{3,2,1,0:T(4,128)} %stack.103), calls=%async_computation.3 | async-start | bytes 2097152 | tf_op jit(solution)/shard_map/all_to_all | solution.py:62
  848.6 183.6 %all-gather.57.cloned.1.call-start = ((), (), s32[]{:S(2)}) async-start(), calls=%async_computation.21 | async-start | bytes 1114112 | tf_op jit(solution)/shard_map/all_gather | solution.py:65
  851.2 200.9 %all-gather.39.cloned.1.call-start = ((), (), s32[]{:S(2)}) async-start(), calls=%async_computation.11 | async-start | bytes 1310720 | tf_op jit(solution)/shard_map/all_gather | solution.py:30
  1027.8 53.1 %all-gather.37.cloned.1.call-start = ((), (), s32[]{:S(2)}) async-start(), calls=%async_computation.9 | async-start | bytes 1310720 | tf_op jit(solution)/shard_map/all_gather | solution.py:30
  1038.4 219.5 %reduce-scatter.5.cloned.1.call-start = ((), (), s32[]{:S(2)}) async-start(), calls=%async_computation.12 | async-start | bytes 4456448 | tf_op jit(solution)/shard_map/reduce_scatter | solution.py:34
  1058.8 203.4 %reduce-scatter.3.cloned.1.call-start = ((), (), s32[]{:S(2)}) async-start(), calls=%async_computation.10 | async-start | bytes 4456448 | tf_op jit(solution)/shard_map/reduce_scatter | solution.py:34
  1158.0 109.3 %copy-start.54 = (f32[1,4,1,32,4,1,128]{6,5,4,3,2,1,0:T(1,128)S(1)}, f32[1,4,1,32,4,1,128]{6,5,4,3,2,1,0:T(1,128)}, u32[]{:S(2)}) copy-start(f32[1,4,1,32,4,1,128]{6,5,4,3,2,1,0:T(1,128)} %param.36) | copy-start | bytes 786436
  1258.0 9.3 collective-permute-start
  (64 other events, 1711.3 us)
Sparse Core Ops, SparseCore 0:
  10.4 42.7 all-gather.40
  55.5 22.6 all-gather.30
  226.5 46.2 all-gather.42
  300.3 22.3 all-gather.32
  479.6 37.5 all-gather.44
  518.9 41.2 all-gather.50
  562.6 22.9 all-gather.34
  587.5 41.6 all-gather.52
  744.9 26.7 all-gather.46
  773.4 45.2 all-gather.54
  820.5 22.5 all-gather.48
  851.4 40.5 all-gather.56
  1027.9 24.2 all-gather.38
  1053.8 27.0 all-gather.36
  1083.2 63.9 reduce-scatter.4
  1149.6 62.5 reduce-scatter.2
